TPU v7x, 256 devices: a whole 4x4x8 slice. The times are simulated.
256 devices in a mesh: tm: 16 (over y, x), space: 16 (over z, core).
Axes of the slice: x: 4, y: 4, z: 8, core: 2. Of those that a mesh axis runs over, the one named last changes fastest.
Arguments:
- stored: bfloat16 [16, 288, 128, 128], P('tm', None, 'space'), may hold values from -6 to 6
- snapshot: int32 [16, 256], P('tm'), may hold values from 0 to 287, as said below
- balance_coef: float32 [128, 128], P('space'), may hold values from 0.5 to 2
- sea_mask: int32 [128, 128], P('space'), may hold values 0 or 1
Outputs:
- merged_basis: bfloat16 [256, 3, 128, 128], P('tm', None, 'space')
Inputs may be any that keep to these rules, and one draw needn't show every extreme that they name: `snapshot`: the 256 indices of one group are distinct.
All inputs are finite; a program needn't handle non-finite values. No bound on the sum of `sea_mask` on one device may be relied on, other than what follows from the above.
Results may differ from a plain program's by a relative error of at most 0.04.
Values may be sent and summed in bfloat16 or wider, within the bound.
No kernel may reach another device: no remote copies, remote signals or barrier semaphores. Data moves between devices by JAX's collectives and lax.ppermute only.
A program may use at most 64 MiB of HBM per device.

v0:
```python
import jax
import jax.numpy as jnp
from jax import lax
from jax.sharding import PartitionSpec as P

inv_root2 = 0.7071067811865476


def gathered_total(shard, axis):
    return lax.all_gather(shard, axis).astype(jnp.float32).sum(0)


def summed_rows(shard, axis):
    count = lax.axis_size(axis)
    parts = lax.all_to_all(shard, axis, 0, 0, tiled=True)
    parts = parts.reshape(count, shard.shape[0] // count, shard.shape[1])
    own_rows = parts.astype(jnp.float32).sum(0)
    return lax.all_gather(own_rows, axis, axis=0, tiled=True)


def with_halo(cells, sides, width):
    for axis, dim in sides:
        count = lax.axis_size(axis)
        ends = count - 1
        head = lax.slice_in_dim(cells, 0, width, axis=dim)
        tail = lax.slice_in_dim(cells, cells.shape[dim] - width, cells.shape[dim], axis=dim)
        cells = jnp.concatenate(
            [
                lax.ppermute(tail, axis, [(i, (i + 1) % count) for i in range(ends)]),
                cells,
                lax.ppermute(head, axis, [((i + 1) % count, i) for i in range(ends)]),
            ],
            axis=dim,
        )
    return cells


def from_partner(shard, axis, stride):
    return lax.ppermute(shard, axis, [(i, i ^ 1 << stride) for i in range(lax.axis_size(axis))])


def balance(padded, balance_coef, sea_float):
    center = padded[:, 1:-1, :]
    cells = lax.broadcasted_iota(jnp.int32, (center.shape[2], center.shape[2]), 0)
    targets = lax.broadcasted_iota(jnp.int32, (center.shape[2], center.shape[2]), 1)
    count = center.shape[2]
    circulant = (cells == (targets + 1) % count).astype(jnp.bfloat16) - (
        cells == (targets - 1) % count
    ).astype(jnp.bfloat16)
    east_minus_west = jnp.einsum(
        "mxy,yz->mxz", center, circulant, preferred_element_type=jnp.float32
    )
    zonal_flow = (-balance_coef * sea_float * east_minus_west).astype(jnp.bfloat16)
    wide = padded.astype(jnp.float32)
    merid_flow = (balance_coef * sea_float * (wide[:, 2:, :] - wide[:, :-2, :])).astype(
        jnp.bfloat16
    )
    return jnp.stack([center, zonal_flow, merid_flow], axis=1).reshape(center.shape[0], -1)


def stack_pair(own_basis, other_basis):
    return jnp.concatenate([own_basis, other_basis], axis=0)


def rotation_of(stacked):
    members = stacked.shape[0] // 2
    local_gram = jnp.dot(stacked, stacked.T, preferred_element_type=jnp.float32)
    local_mixed = (local_gram[:, :members] + local_gram[:, members:]) * inv_root2
    mixed_cols = summed_rows(local_mixed.astype(jnp.bfloat16), "space")
    normal = jnp.dot(
        mixed_cols.T,
        mixed_cols,
        precision=lax.Precision.HIGHEST,
        preferred_element_type=jnp.float32,
    )
    half = normal.shape[0] // 2
    low_11 = lax.linalg.cholesky(normal[:half, :half], symmetrize_input=False)
    low_21 = lax.linalg.triangular_solve(
        low_11, normal[half:, :half], left_side=False, lower=True, transpose_a=True
    )
    low_22 = lax.linalg.cholesky(
        normal[half:, half:] - highest_dot(low_21, low_21.T), symmetrize_input=False
    )
    upper_rows = jax.scipy.linalg.solve_triangular(low_11, mixed_cols[:, :half].T, lower=True)
    lower_rows = jax.scipy.linalg.solve_triangular(
        low_22, mixed_cols[:, half:].T - highest_dot(low_21, upper_rows), lower=True
    )
    return (jnp.concatenate([upper_rows, lower_rows], axis=0) * inv_root2).astype(jnp.bfloat16)


def highest_dot(left, right):
    return jnp.dot(left, right, precision=lax.Precision.HIGHEST, preferred_element_type=jnp.float32)


def rotated(rotation, stacked):
    return jnp.dot(rotation, stacked, preferred_element_type=jnp.float32).astype(jnp.bfloat16)


def body(stored, snapshot, balance_coef, sea_mask):
    sea_float = sea_mask.astype(jnp.float32)
    mean_state = jnp.mean(stored[0].astype(jnp.float32), axis=0)
    picked = jnp.take(stored[0], snapshot[0], axis=0)
    anomaly = ((picked.astype(jnp.float32) - mean_state) * sea_float).astype(jnp.bfloat16)
    other_anomaly = from_partner(anomaly, "tm", 0)
    padded = with_halo(anomaly, (("space", 1),), 1)
    basis_now = balance(padded, balance_coef, sea_float)
    levels = lax.axis_size("tm").bit_length() - 1
    other_rims = from_partner(jnp.concatenate([padded[:, :1], padded[:, -1:]], axis=1), "tm", 0)
    other_padded = jnp.concatenate([other_rims[:, :1], other_anomaly, other_rims[:, 1:]], axis=1)
    partner = balance(other_padded, balance_coef, sea_float)
    stacked = stack_pair(basis_now, partner)
    for level_idx in range(levels):
        if level_idx == levels - 1:
            rotation = rotation_of(stacked)
            member_share = rotation.shape[0] // lax.axis_size("tm")
            rotation = lax.dynamic_slice_in_dim(
                rotation, lax.axis_index("tm") * member_share, member_share, 0
            )
            basis_now = rotated(rotation, stacked)
        else:
            partner_stacked = from_partner(stacked, "tm", level_idx + 1)
            rotation = rotation_of(stacked)
            partner_rotation = from_partner(rotation, "tm", level_idx + 1)
            basis_now = rotated(rotation, stacked)
            partner = rotated(partner_rotation, partner_stacked)
            stacked = stack_pair(basis_now, partner)
    return basis_now.reshape(basis_now.shape[0], 3, stored.shape[2], stored.shape[3])


def solution(mesh):
    placed = (P("tm", None, "space", None), P("tm", None), P("space", None), P("space", None))
    return jax.shard_map(
        body, mesh=mesh, in_specs=placed, out_specs=P("tm", None, "space", None), check_vma=False
    )
```

profile of v0, /device:TPU:1, one launch (start us, length us, event | category | flops | bytes accessed | tf_op | source)
XLA Modules:
  0.0 407.8 jit_solution(4200883872748051215)
XLA Ops:
  27.1 9.4 %all-to-all-start = ((bf16[16,32,256]{2,1,0:T(8,128)(2,1)}), bf16[16,32,256]{2,1,0:T(8,128)(2,1)S(1)}, u32[]{:S(2)}, u32[]{:S(2)}) async-start(bf16[16,32,256]{2,1,0:T(8,128)(2,1)} %bitcast.13), calls=%async_computation | async-start | bytes 524288 | tf_op jit(solution)/shard_map/all_to_all | solution.py:15
  41.2 6.9 %all-to-all-done = bf16[16,32,256]{2,1,0:T(8,128)(2,1)S(1)} async-done(((bf16[16,32,256]{2,1,0:T(8,128)(2,1)}), bf16[16,32,256]{2,1,0:T(8,128)(2,1)S(1)}, u32[]{:S(2)}, u32[]{:S(2)}) %all-to-all-start) | async-done | bytes 262176 | tf_op jit(solution)/shard_map/all_to_all | solution.py:15
  48.1 16.1 %all_gather.12 = f32[512,256]{1,0:T(8,128)S(1)} all-gather(f32[32,256]{1,0:T(8,128)S(1)} %convert_reduce_fusion.4), channel_id=1, replica_groups=mesh['tm'=16,'space'=16] {'space'}, dimensions={0}, use_global_device_ids=true | all-gather | bytes 557056 | tf_op jit(solution)/shard_map/all_gather | solution.py:18
  65.2 11.7 %custom-call.26 = f32[128,128]{1,0:T(8,128)S(1)} custom-call(f32[128,128]{1,0:T(8,128)S(1)} %slice.164), custom_call_target="Cholesky" | custom-call | tf_op jit(solution)/shard_map/cholesky/custom-call.1 | solution.py:77
  78.3 9.8 %custom-call.27 = f32[1,128,128]{1,2,0:T(8,128)S(1)} custom-call(f32[1,128,128]{2,1,0:T(8,128)S(1)} %fusion.27), custom_call_target="InvertDiagBlocksLowerTriangular" | custom-call | tf_op jit(solution)/shard_map/jit(_solve_triangular)/triangular_solve | solution.py:84
  88.7 11.7 %custom-call.29 = f32[128,128]{1,0:T(8,128)S(1)} custom-call(f32[128,128]{1,0:T(8,128)S(1)} %convolution_subtract_fusion.7), custom_call_target="Cholesky" | custom-call | tf_op jit(solution)/shard_map/cholesky/custom-call.1 | solution.py:81
  101.8 10.0 %custom-call.30 = f32[1,128,128]{1,2,0:T(8,128)S(1)} custom-call(f32[1,128,128]{2,1,0:T(8,128)S(1)} %fusion.28), custom_call_target="InvertDiagBlocksLowerTriangular" | custom-call | tf_op jit(solution)/shard_map/jit(_solve_triangular)/triangular_solve | solution.py:85
  137.3 8.4 %all-to-all-done.1 = bf16[16,32,256]{2,1,0:T(8,128)(2,1)S(1)} async-done(((bf16[16,32,256]{2,1,0:T(8,128)(2,1)}), bf16[16,32,256]{2,1,0:T(8,128)(2,1)S(1)}, u32[]{:S(2)}, u32[]{:S(2)}) %all-to-all-start.1) | async-done | bytes 262176 | tf_op jit(solution)/shard_map/all_to_all | solution.py:15
  145.8 16.3 %all_gather.13 = f32[512,256]{1,0:T(8,128)S(1)} all-gather(f32[32,256]{1,0:T(8,128)S(1)} %convert_reduce_fusion.3), channel_id=1, replica_groups=mesh['tm'=16,'space'=16] {'space'}, dimensions={0}, use_global_device_ids=true | all-gather | bytes 557056 | tf_op jit(solution)/shard_map/all_gather | solution.py:18
  163.1 11.7 %custom-call.31 = f32[128,128]{1,0:T(8,128)S(1)} custom-call(f32[128,128]{1,0:T(8,128)S(1)} %slice.171), custom_call_target="Cholesky" | custom-call | tf_op jit(solution)/shard_map/cholesky/custom-call.1 | solution.py:77
  176.2 9.8 %custom-call.32 = f32[1,128,128]{1,2,0:T(8,128)S(1)} custom-call(f32[1,128,128]{2,1,0:T(8,128)S(1)} %fusion.29), custom_call_target="InvertDiagBlocksLowerTriangular" | custom-call | tf_op jit(solution)/shard_map/jit(_solve_triangular)/triangular_solve | solution.py:84
  186.6 11.7 %custom-call.34 = f32[128,128]{1,0:T(8,128)S(1)} custom-call(f32[128,128]{1,0:T(8,128)S(1)} %convolution_subtract_fusion.6), custom_call_target="Cholesky" | custom-call | tf_op jit(solution)/shard_map/cholesky/custom-call.1 | solution.py:81
  199.6 9.9 %custom-call.35 = f32[1,128,128]{1,2,0:T(8,128)S(1)} custom-call(f32[1,128,128]{2,1,0:T(8,128)S(1)} %fusion.30), custom_call_target="InvertDiagBlocksLowerTriangular" | custom-call | tf_op jit(solution)/shard_map/jit(_solve_triangular)/triangular_solve | solution.py:85
  242.1 16.1 %all_gather.14 = f32[512,256]{1,0:T(8,128)S(1)} all-gather(f32[32,256]{1,0:T(8,128)S(1)} %convert_reduce_fusion.2), channel_id=1, replica_groups=mesh['tm'=16,'space'=16] {'space'}, dimensions={0}, use_global_device_ids=true | all-gather | bytes 557056 | tf_op jit(solution)/shard_map/all_gather | solution.py:18
  259.2 11.7 %custom-call.36 = f32[128,128]{1,0:T(8,128)S(1)} custom-call(f32[128,128]{1,0:T(8,128)S(1)} %slice.178), custom_call_target="Cholesky" | custom-call | tf_op jit(solution)/shard_map/cholesky/custom-call.1 | solution.py:77
  272.3 9.8 %custom-call.37 = f32[1,128,128]{1,2,0:T(8,128)S(1)} custom-call(f32[1,128,128]{2,1,0:T(8,128)S(1)} %fusion.31), custom_call_target="InvertDiagBlocksLowerTriangular" | custom-call | tf_op jit(solution)/shard_map/jit(_solve_triangular)/triangular_solve | solution.py:84
  282.7 11.7 %custom-call.39 = f32[128,128]{1,0:T(8,128)S(1)} custom-call(f32[128,128]{1,0:T(8,128)S(1)} %convolution_subtract_fusion.5), custom_call_target="Cholesky" | custom-call | tf_op jit(solution)/shard_map/cholesky/custom-call.1 | solution.py:81
  295.7 10.2 %custom-call.40 = f32[1,128,128]{1,2,0:T(8,128)S(1)} custom-call(f32[1,128,128]{2,1,0:T(8,128)S(1)} %fusion.32), custom_call_target="InvertDiagBlocksLowerTriangular" | custom-call | tf_op jit(solution)/shard_map/jit(_solve_triangular)/triangular_solve | solution.py:85
  328.3 11.6 %all-to-all-done.3 = bf16[16,32,256]{2,1,0:T(8,128)(2,1)S(1)} async-done(((bf16[16,32,256]{2,1,0:T(8,128)(2,1)}), bf16[16,32,256]{2,1,0:T(8,128)(2,1)S(1)}, u32[]{:S(2)}, u32[]{:S(2)}) %all-to-all-start.3) | async-done | bytes 262176 | tf_op jit(solution)/shard_map/all_to_all | solution.py:15
  340.0 16.1 %all_gather.15 = f32[512,256]{1,0:T(8,128)S(1)} all-gather(f32[32,256]{1,0:T(8,128)S(1)} %convert_reduce_fusion.1), channel_id=1, replica_groups=mesh['tm'=16,'space'=16] {'space'}, dimensions={0}, use_global_device_ids=true | all-gather | bytes 557056 | tf_op jit(solution)/shard_map/all_gather | solution.py:18
  357.1 11.7 %custom-call.41 = f32[128,128]{1,0:T(8,128)S(1)} custom-call(f32[128,128]{1,0:T(8,128)S(1)} %slice.185), custom_call_target="Cholesky" | custom-call | tf_op jit(solution)/shard_map/cholesky/custom-call.1 | solution.py:77
  370.1 9.8 %custom-call.42 = f32[1,128,128]{1,2,0:T(8,128)S(1)} custom-call(f32[1,128,128]{2,1,0:T(8,128)S(1)} %fusion.33), custom_call_target="InvertDiagBlocksLowerTriangular" | custom-call | tf_op jit(solution)/shard_map/jit(_solve_triangular)/triangular_solve | solution.py:84
  381.0 11.7 %custom-call.44 = f32[128,128]{1,0:T(8,128)S(1)} custom-call(f32[128,128]{1,0:T(8,128)S(1)} %convolution_subtract_fusion.4), custom_call_target="Cholesky" | custom-call | tf_op jit(solution)/shard_map/cholesky/custom-call.1 | solution.py:81
  394.0 10.0 %custom-call.45 = f32[1,128,128]{1,2,0:T(8,128)S(1)} custom-call(f32[1,128,128]{2,1,0:T(8,128)S(1)} %fusion.34), custom_call_target="InvertDiagBlocksLowerTriangular" | custom-call | tf_op jit(solution)/shard_map/jit(_solve_triangular)/triangular_solve | solution.py:85
  (140 shorter events, 133.0 us)
Async XLA Ops:
  0.0 14.9 %copy-start.3 = (s32[8,128]{1,0:T(8,128)S(1)}, s32[8,128]{1,0:T(8,128)}, u32[]{:S(2)}) copy-start(s32[8,128]{1,0:T(8,128)} %param.12) | copy-start | bytes 12292
  0.0 14.9 %copy-start.4 = (f32[8,128]{1,0:T(8,128)S(1)}, f32[8,128]{1,0:T(8,128)}, u32[]{:S(2)}) copy-start(f32[8,128]{1,0:T(8,128)} %param.11) | copy-start | bytes 12292
  6.1 17.1 %collective-permute-start.2 = (bf16[256,8,128]{0,2,1:T(8,128)(2,1)S(1)}, bf16[256,8,128]{0,2,1:T(8,128)(2,1)S(1)}, u32[]{:S(2)}, u32[]{:S(2)}) collective-permute-start(bf16[256,8,128]{0,2,1:T(8,128)(2,1)S(1)} %multiply_convert_fusion), channel_id=1, source_target_pairs={{0,16},{16,0},{32,48},{48,32},{64,80},{80,64},{96,112},{112,96},{1... | collective-permute-start | bytes 1572872 | tf_op jit(solution)/shard_map/ppermute | solution.py:39
  8.2 7.2 %collective-permute-start = (bf16[256,1,128]{0,2,1:T(8,128)(2,1)S(1)}, bf16[256,1,128]{0,2,1:T(8,128)(2,1)S(1)}, u32[]{:S(2)}, u32[]{:S(2)}) collective-permute-start(bf16[256,1,128]{0,2,1:T(8,128)(2,1)S(1)} %get-tuple-element.6), channel_id=1, source_target_pairs={{0,1},{1,2},{2,3},{3,4},{4,5},{5,6},{6,7},{7,8},{8,9},{9,10},{10,1... | collective-permute-start | bytes 196616 | tf_op jit(solution)/shard_map/ppermute | solution.py:29
  12.6 5.9 %collective-permute-start.1 = (bf16[256,1,128]{0,2,1:T(8,128)(2,1)S(1)}, bf16[256,1,128]{0,2,1:T(8,128)(2,1)S(1)}, u32[]{:S(2)}, u32[]{:S(2)}) collective-permute-start(bf16[256,1,128]{0,2,1:T(8,128)(2,1)S(1)} %get-tuple-element.8), channel_id=1, source_target_pairs={{1,0},{2,1},{3,2},{4,3},{5,4},{6,5},{7,6},{8,7},{9,8},{10,9},{11,1... | collective-permute-start | bytes 196616 | tf_op jit(solution)/shard_map/ppermute | solution.py:31
  18.5 4.7 %collective-permute-start.3 = (bf16[256,2,128]{0,2,1:T(8,128)(2,1)S(1)}, bf16[256,2,128]{0,2,1:T(8,128)(2,1)S(1)}, u32[]{:S(2)}, u32[]{:S(2)}) collective-permute-start(bf16[256,2,128]{0,2,1:T(8,128)(2,1)S(1)} %pad_maximum_fusion.10), channel_id=1, source_target_pairs={{0,16},{16,0},{32,48},{48,32},{64,80},{80,64},{96,112},{112,96},{1... | collective-permute-start | bytes 393224 | tf_op jit(solution)/shard_map/ppermute | solution.py:39
  24.5 12.0 %copy-start = (bf16[256,3,8,128]{0,3,2,1:T(8,128)(2,1)}, bf16[256,3,8,128]{0,3,2,1:T(8,128)(2,1)S(1)}, u32[]{:S(2)}) copy-start(bf16[256,3,8,128]{0,3,2,1:T(8,128)(2,1)S(1)} %get-tuple-element.17) | copy-start | bytes 4718596
  27.1 21.0 %all-to-all-start = ((bf16[16,32,256]{2,1,0:T(8,128)(2,1)}), bf16[16,32,256]{2,1,0:T(8,128)(2,1)S(1)}, u32[]{:S(2)}, u32[]{:S(2)}) async-start(bf16[16,32,256]{2,1,0:T(8,128)(2,1)} %bitcast.13), calls=%async_computation | async-start | bytes 524288 | tf_op jit(solution)/shard_map/all_to_all | solution.py:15
  38.4 84.1 %collective-permute-start.5 = (bf16[512,3072]{0,1:T(8,128)(2,1)}, bf16[512,3072]{0,1:T(8,128)(2,1)}, u32[]{:S(2)}, u32[]{:S(2)}) collective-permute-start(bf16[512,3072]{0,1:T(8,128)(2,1)} %pad_maximum_fusion), channel_id=1, source_target_pairs={{0,32},{16,48},{32,0},{48,16},{64,96},{80,112},{96,64},{112,80},{1... | collective-permute-start | bytes 9437192 | tf_op jit(solution)/shard_map/ppermute | solution.py:39
  113.2 9.3 %collective-permute-start.4 = (bf16[256,512]{1,0:T(8,128)(2,1)S(1)}, bf16[256,512]{1,0:T(8,128)(2,1)S(1)}, u32[]{:S(2)}, u32[]{:S(2)}) collective-permute-start(bf16[256,512]{1,0:T(8,128)(2,1)S(1)} %fusion.20), channel_id=1, source_target_pairs={{0,32},{16,48},{32,0},{48,16},{64,96},{80,112},{96,64},{112,80},{1... | collective-permute-start | bytes 786440 | tf_op jit(solution)/shard_map/ppermute | solution.py:39
  118.5 15.6 %copy-start.1 = (bf16[256,3072]{1,0:T(8,128)(2,1)}, bf16[256,3072]{1,0:T(8,128)(2,1)S(1)}, u32[]{:S(2)}) copy-start(bf16[256,3072]{1,0:T(8,128)(2,1)S(1)} %convolution_convert_fusion.5) | copy-start | bytes 4718596
  128.0 17.7 %all-to-all-start.1 = ((bf16[16,32,256]{2,1,0:T(8,128)(2,1)}), bf16[16,32,256]{2,1,0:T(8,128)(2,1)S(1)}, u32[]{:S(2)}, u32[]{:S(2)}) async-start(bf16[16,32,256]{2,1,0:T(8,128)(2,1)} %bitcast.23), calls=%async_computation.1 | async-start | bytes 524288 | tf_op jit(solution)/shard_map/all_to_all | solution.py:15
  136.0 82.8 %collective-permute-start.7 = (bf16[512,3072]{1,0:T(8,128)(2,1)}, bf16[512,3072]{1,0:T(8,128)(2,1)}, u32[]{:S(2)}, u32[]{:S(2)}) collective-permute-start(bf16[512,3072]{1,0:T(8,128)(2,1)} %pad_maximum_fusion.1), channel_id=1, source_target_pairs={{0,64},{16,80},{32,96},{48,112},{64,0},{80,16},{96,32},{112,48},{1... | collective-permute-start | bytes 9437192 | tf_op jit(solution)/shard_map/ppermute | solution.py:39
  211.1 7.8 %collective-permute-start.6 = (bf16[256,512]{1,0:T(8,128)(2,1)S(1)}, bf16[256,512]{1,0:T(8,128)(2,1)S(1)}, u32[]{:S(2)}, u32[]{:S(2)}) collective-permute-start(bf16[256,512]{1,0:T(8,128)(2,1)S(1)} %fusion.21), channel_id=1, source_target_pairs={{0,64},{16,80},{32,96},{48,112},{64,0},{80,16},{96,32},{112,48},{1... | collective-permute-start | bytes 786440 | tf_op jit(solution)/shard_map/ppermute | solution.py:39
  214.9 15.6 %copy-start.2 = (bf16[256,3072]{1,0:T(8,128)(2,1)}, bf16[256,3072]{1,0:T(8,128)(2,1)S(1)}, u32[]{:S(2)}) copy-start(bf16[256,3072]{1,0:T(8,128)(2,1)S(1)} %convolution_convert_fusion.3) | copy-start | bytes 4718596
  224.4 17.7 %all-to-all-start.2 = ((bf16[16,32,256]{2,1,0:T(8,128)(2,1)}), bf16[16,32,256]{2,1,0:T(8,128)(2,1)S(1)}, u32[]{:S(2)}, u32[]{:S(2)}) async-start(bf16[16,32,256]{2,1,0:T(8,128)(2,1)} %bitcast.33), calls=%async_computation.2 | async-start | bytes 524288 | tf_op jit(solution)/shard_map/all_to_all | solution.py:15
  232.3 84.4 %collective-permute-start.9 = (bf16[512,3072]{1,0:T(8,128)(2,1)}, bf16[512,3072]{1,0:T(8,128)(2,1)}, u32[]{:S(2)}, u32[]{:S(2)}) collective-permute-start(bf16[512,3072]{1,0:T(8,128)(2,1)} %pad_maximum_fusion.2), channel_id=1, source_target_pairs={{0,128},{16,144},{32,160},{48,176},{64,192},{80,208},{96,224},{112... | collective-permute-start | bytes 9437192 | tf_op jit(solution)/shard_map/ppermute | solution.py:39
  307.4 9.3 %collective-permute-start.8 = (bf16[256,512]{1,0:T(8,128)(2,1)S(1)}, bf16[256,512]{1,0:T(8,128)(2,1)S(1)}, u32[]{:S(2)}, u32[]{:S(2)}) collective-permute-start(bf16[256,512]{1,0:T(8,128)(2,1)S(1)} %fusion.22), channel_id=1, source_target_pairs={{0,128},{16,144},{32,160},{48,176},{64,192},{80,208},{96,224},{112... | collective-permute-start | bytes 786440 | tf_op jit(solution)/shard_map/ppermute | solution.py:39
  312.8 8.7 %copy-start.5 = (bf16[256,3072]{1,0:T(8,128)(2,1)}, bf16[256,3072]{1,0:T(8,128)(2,1)S(1)}, u32[]{:S(2)}) copy-start(bf16[256,3072]{1,0:T(8,128)(2,1)S(1)} %convolution_convert_fusion.1) | copy-start | bytes 4718596
  322.3 17.7 %all-to-all-start.3 = ((bf16[16,32,256]{2,1,0:T(8,128)(2,1)}), bf16[16,32,256]{2,1,0:T(8,128)(2,1)S(1)}, u32[]{:S(2)}, u32[]{:S(2)}) async-start(bf16[16,32,256]{2,1,0:T(8,128)(2,1)} %bitcast.43), calls=%async_computation.3 | async-start | bytes 524288 | tf_op jit(solution)/shard_map/all_to_all | solution.py:15
where the time goes:
time: 414 us; the launch traced here: 408 us
  other arithmetic  198 us (48%)
  blocking collectives  64.6 us (16%)
  waiting for transfers between devices  52.9 us (13%)
  starting transfers between devices  50.6 us (12%)
  matrix products  38 us (9%)
    all_gather x4, blocking collectives, summed_rows(): return lax.all_gather(own_rows, axis, axis=0, tiled=True)  64.6 us
    another operation x12, other arithmetic, rotation_of(): lax.linalg.cholesky(normal[half:, half:] - highest_dot(low_21, low_21.T),...  49.6 us
    another operation x12, other arithmetic, rotation_of(): low_11 = lax.linalg.cholesky(normal[:half, :half], symmetrize_input=False)  49.6 us
    another operation x8, other arithmetic, rotation_of(): jax.scipy.linalg.solve_triangular(low_22, mixed_cols[:, half:].T - highes...  42.7 us
    another operation x8, other arithmetic, rotation_of(): jax.scipy.linalg.solve_triangular(low_11, mixed_cols[:, :half].T, lower=T...  41.9 us
    all_to_all x4, waiting for transfers between devices, summed_rows(): parts = lax.all_to_all(shard, axis, 0, 0, tiled=True)  33.7 us
    all_to_all x4, starting transfers between devices, summed_rows(): parts = lax.all_to_all(shard, axis, 0, 0, tiled=True)  27.7 us
    dot_general x7, matrix products, rotated(): jnp.dot(rotation, stacked, preferred_element_type=jnp.float32)  17.9 us
  transfers between devices with their start and end apart: 14, of which 9 were waited for; matrix products, arithmetic and copies ran while one was open for 39% of the time, Pallas kernels for 0%

commit v1 on v0

--- a/solution.py
+++ b/solution.py
@@ -15,7 +15,9 @@
     parts = lax.all_to_all(shard, axis, 0, 0, tiled=True)
     parts = parts.reshape(count, shard.shape[0] // count, shard.shape[1])
     own_rows = parts.astype(jnp.float32).sum(0)
-    return lax.all_gather(own_rows, axis, axis=0, tiled=True)
+    return jnp.concatenate(
+        lax.all_to_all(jnp.stack([own_rows] * lax.axis_size(axis)), axis, 0, 0), axis=0
+    )
 
 
 def with_halo(cells, sides, width):

time: 414 us -> 450 us (1.087)
  waiting for transfers between devices: 52.9 us -> 82.3 us
  starting transfers between devices: 50.6 us -> 38.4 us
  blocking collectives: 64.6 us -> 74.2 us
    all_to_all x0 -> x4, blocking collectives: none -> 74.2 us  [summed_rows(): parts = lax.all_to_all(shard, axis, 0, 0, tiled=True)]
    all_gather x4 -> x0, blocking collectives: 64.6 us -> none  [summed_rows(): return lax.all_gather(own_rows, axis, axis=0, tiled=True)]
    all_to_all x4, waiting for transfers between devices: 33.7 us -> 50.7 us  [summed_rows(): lax.all_to_all(jnp.stack([own_rows] * lax.axis_size(axis)), axis, 0, 0)]
    all_to_all x4, starting transfers between devices: 27.7 us -> 14.7 us  [summed_rows(): lax.all_to_all(jnp.stack([own_rows] * lax.axis_size(axis)), axis, 0, 0)]
    ppermute x8, waiting for transfers between devices: 16.1 us -> 28.5 us  [from_partner(): lax.ppermute(shard, axis, [(i, i ^ 1 << stride) for i in range(lax.axis_s...]
  transfers between devices with their start and end apart: 14 -> 14, of which waited for: 9 -> 9; matrix products, arithmetic and copies ran while one was open for 39% -> 38% of each run, Pallas kernels for 0% -> 0%
where the time goes in v1:
time: 450 us; the launch traced here: 443 us
  other arithmetic  200 us (44%)
  waiting for transfers between devices  82.3 us (18%)
  blocking collectives  74.2 us (16%)
  matrix products  40.5 us (9%)
  starting transfers between devices  38.4 us (9%)
  local copies, waits for them, and re-layouts  6.38 us (1%)
    all_to_all x4, blocking collectives, summed_rows(): parts = lax.all_to_all(shard, axis, 0, 0, tiled=True)  74.2 us
    all_to_all x4, waiting for transfers between devices, summed_rows(): lax.all_to_all(jnp.stack([own_rows] * lax.axis_size(axis)), axis, 0, 0)  50.7 us
    another operation x12, other arithmetic, rotation_of(): lax.linalg.cholesky(normal[half:, half:] - highest_dot(low_21, low_21.T),...  50.4 us
    another operation x12, other arithmetic, rotation_of(): low_11 = lax.linalg.cholesky(normal[:half, :half], symmetrize_input=False)  49.6 us
    another operation x8, other arithmetic, rotation_of(): jax.scipy.linalg.solve_triangular(low_11, mixed_cols[:, :half].T, lower=T...  43.4 us
    another operation x8, other arithmetic, rotation_of(): jax.scipy.linalg.solve_triangular(low_22, mixed_cols[:, half:].T - highes...  42.8 us
    ppermute x8, waiting for transfers between devices, from_partner(): lax.ppermute(shard, axis, [(i, i ^ 1 << stride) for i in range(lax.axis_s...  28.5 us
    ppermute x8, starting transfers between devices, from_partner(): lax.ppermute(shard, axis, [(i, i ^ 1 << stride) for i in range(lax.axis_s...  17.4 us
  transfers between devices with their start and end apart: 14, of which 9 were waited for; matrix products, arithmetic and copies ran while one was open for 38% of the time, Pallas kernels for 0%

profile of v1, /device:TPU:1, one launch (start us, length us, event | category | flops | bytes accessed | tf_op | source)
XLA Modules:
  0.0 443.1 jit_solution(6219807550375363598)
XLA Ops:
  26.4 20.8 %all_to_all.56 = bf16[16,32,256]{2,1,0:T(8,128)(2,1)S(1)} all-to-all(bf16[16,32,256]{2,1,0:T(8,128)(2,1)S(1)} %bitcast.190), channel_id=1, replica_groups=mesh['tm'=16,'space'=16] {'space'}, dimensions={0} | all-to-all | bytes 524288 | tf_op jit(solution)/shard_map/all_to_all | solution.py:15
  57.0 12.0 %all-to-all-done.1 = f32[16,32,256]{2,1,0:T(8,128)} async-done(((f32[16,32,256]{2,1,0:T(8,128)}), f32[16,32,256]{2,1,0:T(8,128)}, u32[]{:S(2)}, u32[]{:S(2)}) %all-to-all-start.1) | async-done | bytes 524320 | tf_op jit(solution)/shard_map/all_to_all | solution.py:19
  71.3 11.7 %custom-call.26 = f32[128,128]{1,0:T(8,128)S(1)} custom-call(f32[128,128]{1,0:T(8,128)S(1)} %slice.164), custom_call_target="Cholesky" | custom-call | tf_op jit(solution)/shard_map/cholesky/custom-call.1 | solution.py:79
  85.1 10.6 %custom-call.27 = f32[1,128,128]{1,2,0:T(8,128)S(1)} custom-call(f32[1,128,128]{2,1,0:T(8,128)} %fusion.27), custom_call_target="InvertDiagBlocksLowerTriangular" | custom-call | tf_op jit(solution)/shard_map/jit(_solve_triangular)/triangular_solve | solution.py:86
  96.9 12.5 %custom-call.29 = f32[128,128]{1,0:T(8,128)S(1)} custom-call(f32[128,128]{1,0:T(8,128)} %convolution_subtract_fusion.7), custom_call_target="Cholesky" | custom-call | tf_op jit(solution)/shard_map/cholesky/custom-call.1 | solution.py:83
  110.8 10.0 %custom-call.30 = f32[1,128,128]{1,2,0:T(8,128)S(1)} custom-call(f32[1,128,128]{2,1,0:T(8,128)S(1)} %fusion.28), custom_call_target="InvertDiagBlocksLowerTriangular" | custom-call | tf_op jit(solution)/shard_map/jit(_solve_triangular)/triangular_solve | solution.py:87
  138.1 16.6 %all_to_all.57 = bf16[16,32,256]{2,1,0:T(8,128)(2,1)S(1)} all-to-all(bf16[16,32,256]{2,1,0:T(8,128)(2,1)S(1)} %bitcast.191), channel_id=1, replica_groups=mesh['tm'=16,'space'=16] {'space'}, dimensions={0} | all-to-all | bytes 524288 | tf_op jit(solution)/shard_map/all_to_all | solution.py:15
  164.1 11.8 %all-to-all-done.3 = f32[16,32,256]{2,1,0:T(8,128)S(1)} async-done(((f32[16,32,256]{2,1,0:T(8,128)}), f32[16,32,256]{2,1,0:T(8,128)S(1)}, u32[]{:S(2)}, u32[]{:S(2)}) %all-to-all-start.3) | async-done | bytes 524320 | tf_op jit(solution)/shard_map/all_to_all | solution.py:19
  176.9 11.7 %custom-call.31 = f32[128,128]{1,0:T(8,128)S(1)} custom-call(f32[128,128]{1,0:T(8,128)S(1)} %slice.171), custom_call_target="Cholesky" | custom-call | tf_op jit(solution)/shard_map/cholesky/custom-call.1 | solution.py:79
  190.0 9.8 %custom-call.32 = f32[1,128,128]{1,2,0:T(8,128)S(1)} custom-call(f32[1,128,128]{2,1,0:T(8,128)S(1)} %fusion.29), custom_call_target="InvertDiagBlocksLowerTriangular" | custom-call | tf_op jit(solution)/shard_map/jit(_solve_triangular)/triangular_solve | solution.py:86
  200.4 11.7 %custom-call.34 = f32[128,128]{1,0:T(8,128)S(1)} custom-call(f32[128,128]{1,0:T(8,128)S(1)} %convolution_subtract_fusion.6), custom_call_target="Cholesky" | custom-call | tf_op jit(solution)/shard_map/cholesky/custom-call.1 | solution.py:83
  213.4 10.0 %custom-call.35 = f32[1,128,128]{1,2,0:T(8,128)S(1)} custom-call(f32[1,128,128]{2,1,0:T(8,128)S(1)} %fusion.30), custom_call_target="InvertDiagBlocksLowerTriangular" | custom-call | tf_op jit(solution)/shard_map/jit(_solve_triangular)/triangular_solve | solution.py:87
  243.3 18.4 %all_to_all.58 = bf16[16,32,256]{2,1,0:T(8,128)(2,1)S(1)} all-to-all(bf16[16,32,256]{2,1,0:T(8,128)(2,1)S(1)} %bitcast.192), channel_id=1, replica_groups=mesh['tm'=16,'space'=16] {'space'}, dimensions={0} | all-to-all | bytes 524288 | tf_op jit(solution)/shard_map/all_to_all | solution.py:15
  272.5 10.4 %all-to-all-done.5 = f32[16,32,256]{2,1,0:T(8,128)S(1)} async-done(((f32[16,32,256]{2,1,0:T(8,128)}), f32[16,32,256]{2,1,0:T(8,128)S(1)}, u32[]{:S(2)}, u32[]{:S(2)}) %all-to-all-start.5) | async-done | bytes 524320 | tf_op jit(solution)/shard_map/all_to_all | solution.py:19
  283.9 11.7 %custom-call.36 = f32[128,128]{1,0:T(8,128)S(1)} custom-call(f32[128,128]{1,0:T(8,128)S(1)} %slice.178), custom_call_target="Cholesky" | custom-call | tf_op jit(solution)/shard_map/cholesky/custom-call.1 | solution.py:79
  297.0 9.8 %custom-call.37 = f32[1,128,128]{1,2,0:T(8,128)S(1)} custom-call(f32[1,128,128]{2,1,0:T(8,128)S(1)} %fusion.31), custom_call_target="InvertDiagBlocksLowerTriangular" | custom-call | tf_op jit(solution)/shard_map/jit(_solve_triangular)/triangular_solve | solution.py:86
  307.4 11.7 %custom-call.39 = f32[128,128]{1,0:T(8,128)S(1)} custom-call(f32[128,128]{1,0:T(8,128)S(1)} %convolution_subtract_fusion.5), custom_call_target="Cholesky" | custom-call | tf_op jit(solution)/shard_map/cholesky/custom-call.1 | solution.py:83
  320.5 10.2 %custom-call.40 = f32[1,128,128]{1,2,0:T(8,128)S(1)} custom-call(f32[1,128,128]{2,1,0:T(8,128)S(1)} %fusion.32), custom_call_target="InvertDiagBlocksLowerTriangular" | custom-call | tf_op jit(solution)/shard_map/jit(_solve_triangular)/triangular_solve | solution.py:87
  351.7 18.4 %all_to_all.59 = bf16[16,32,256]{2,1,0:T(8,128)(2,1)S(1)} all-to-all(bf16[16,32,256]{2,1,0:T(8,128)(2,1)S(1)} %bitcast.193), channel_id=1, replica_groups=mesh['tm'=16,'space'=16] {'space'}, dimensions={0} | all-to-all | bytes 524288 | tf_op jit(solution)/shard_map/all_to_all | solution.py:15
  374.7 16.6 %all-to-all-done.7 = f32[16,32,256]{2,1,0:T(8,128)S(1)} async-done(((f32[16,32,256]{2,1,0:T(8,128)}), f32[16,32,256]{2,1,0:T(8,128)S(1)}, u32[]{:S(2)}, u32[]{:S(2)}) %all-to-all-start.7) | async-done | bytes 524320 | tf_op jit(solution)/shard_map/all_to_all | solution.py:19
  392.3 11.7 %custom-call.41 = f32[128,128]{1,0:T(8,128)S(1)} custom-call(f32[128,128]{1,0:T(8,128)S(1)} %slice.185), custom_call_target="Cholesky" | custom-call | tf_op jit(solution)/shard_map/cholesky/custom-call.1 | solution.py:79
  405.3 9.8 %custom-call.42 = f32[1,128,128]{1,2,0:T(8,128)S(1)} custom-call(f32[1,128,128]{2,1,0:T(8,128)S(1)} %fusion.33), custom_call_target="InvertDiagBlocksLowerTriangular" | custom-call | tf_op jit(solution)/shard_map/jit(_solve_triangular)/triangular_solve | solution.py:86
  415.7 11.7 %custom-call.44 = f32[128,128]{1,0:T(8,128)S(1)} custom-call(f32[128,128]{1,0:T(8,128)S(1)} %convolution_subtract_fusion.4), custom_call_target="Cholesky" | custom-call | tf_op jit(solution)/shard_map/cholesky/custom-call.1 | solution.py:83
  428.8 10.0 %custom-call.45 = f32[1,128,128]{1,2,0:T(8,128)S(1)} custom-call(f32[1,128,128]{2,1,0:T(8,128)S(1)} %fusion.34), custom_call_target="InvertDiagBlocksLowerTriangular" | custom-call | tf_op jit(solution)/shard_map/jit(_solve_triangular)/triangular_solve | solution.py:87
  (142 shorter events, 142.4 us)
Async XLA Ops:
  0.0 14.9 %copy-start.2 = (s32[8,128]{1,0:T(8,128)S(1)}, s32[8,128]{1,0:T(8,128)}, u32[]{:S(2)}) copy-start(s32[8,128]{1,0:T(8,128)} %param.12) | copy-start | bytes 12292
  0.0 14.9 %copy-start.3 = (f32[8,128]{1,0:T(8,128)S(1)}, f32[8,128]{1,0:T(8,128)}, u32[]{:S(2)}) copy-start(f32[8,128]{1,0:T(8,128)} %param.11) | copy-start | bytes 12292
  6.0 17.1 %collective-permute-start.2 = (bf16[256,8,128]{0,2,1:T(8,128)(2,1)S(1)}, bf16[256,8,128]{0,2,1:T(8,128)(2,1)S(1)}, u32[]{:S(2)}, u32[]{:S(2)}) collective-permute-start(bf16[256,8,128]{0,2,1:T(8,128)(2,1)S(1)} %multiply_convert_fusion), channel_id=1, source_target_pairs={{0,16},{16,0},{32,48},{48,32},{64,80},{80,64},{96,112},{112,96},{1... | collective-permute-start | bytes 1572872 | tf_op jit(solution)/shard_map/ppermute | solution.py:41
  8.2 7.2 %collective-permute-start = (bf16[256,1,128]{0,2,1:T(8,128)(2,1)S(1)}, bf16[256,1,128]{0,2,1:T(8,128)(2,1)S(1)}, u32[]{:S(2)}, u32[]{:S(2)}) collective-permute-start(bf16[256,1,128]{0,2,1:T(8,128)(2,1)S(1)} %get-tuple-element.6), channel_id=1, source_target_pairs={{0,1},{1,2},{2,3},{3,4},{4,5},{5,6},{6,7},{7,8},{8,9},{9,10},{10,1... | collective-permute-start | bytes 196616 | tf_op jit(solution)/shard_map/ppermute | solution.py:31
  12.6 5.9 %collective-permute-start.1 = (bf16[256,1,128]{0,2,1:T(8,128)(2,1)S(1)}, bf16[256,1,128]{0,2,1:T(8,128)(2,1)S(1)}, u32[]{:S(2)}, u32[]{:S(2)}) collective-permute-start(bf16[256,1,128]{0,2,1:T(8,128)(2,1)S(1)} %get-tuple-element.8), channel_id=1, source_target_pairs={{1,0},{2,1},{3,2},{4,3},{5,4},{6,5},{7,6},{8,7},{9,8},{10,9},{11,1... | collective-permute-start | bytes 196616 | tf_op jit(solution)/shard_map/ppermute | solution.py:33
  18.5 4.7 %collective-permute-start.3 = (bf16[256,2,128]{0,2,1:T(8,128)(2,1)S(1)}, bf16[256,2,128]{0,2,1:T(8,128)(2,1)S(1)}, u32[]{:S(2)}, u32[]{:S(2)}) collective-permute-start(bf16[256,2,128]{0,2,1:T(8,128)(2,1)S(1)} %pad_maximum_fusion.10), channel_id=1, source_target_pairs={{0,16},{16,0},{32,48},{48,32},{64,80},{80,64},{96,112},{112,96},{1... | collective-permute-start | bytes 393224 | tf_op jit(solution)/shard_map/ppermute | solution.py:41
  48.1 20.9 %all-to-all-start.1 = ((f32[16,32,256]{2,1,0:T(8,128)}), f32[16,32,256]{2,1,0:T(8,128)}, u32[]{:S(2)}, u32[]{:S(2)}) async-start(f32[16,32,256]{2,1,0:T(8,128)} %stack.29), calls=%async_computation.1 | async-start | bytes 1048576 | tf_op jit(solution)/shard_map/all_to_all | solution.py:19
  54.1 79.2 %collective-permute-start.5 = (bf16[512,3072]{0,1:T(8,128)(2,1)}, bf16[512,3072]{0,1:T(8,128)(2,1)}, u32[]{:S(2)}, u32[]{:S(2)}) collective-permute-start(bf16[512,3072]{0,1:T(8,128)(2,1)} %pad_maximum_fusion), channel_id=1, source_target_pairs={{0,32},{16,48},{32,0},{48,16},{64,96},{80,112},{96,64},{112,80},{1... | collective-permute-start | bytes 9437192 | tf_op jit(solution)/shard_map/ppermute | solution.py:41
  124.2 9.1 %collective-permute-start.4 = (bf16[256,512]{1,0:T(8,128)(2,1)S(1)}, bf16[256,512]{1,0:T(8,128)(2,1)S(1)}, u32[]{:S(2)}, u32[]{:S(2)}) collective-permute-start(bf16[256,512]{1,0:T(8,128)(2,1)S(1)} %fusion.20), channel_id=1, source_target_pairs={{0,32},{16,48},{32,0},{48,16},{64,96},{80,112},{96,64},{112,80},{1... | collective-permute-start | bytes 786440 | tf_op jit(solution)/shard_map/ppermute | solution.py:41
  128.1 10.0 %copy-start = (bf16[256,3072]{1,0:T(8,128)(2,1)}, bf16[256,3072]{1,0:T(8,128)(2,1)S(1)}, u32[]{:S(2)}) copy-start(bf16[256,3072]{1,0:T(8,128)(2,1)S(1)} %convolution_convert_fusion.5) | copy-start | bytes 4718596
  155.6 20.2 %all-to-all-start.3 = ((f32[16,32,256]{2,1,0:T(8,128)}), f32[16,32,256]{2,1,0:T(8,128)S(1)}, u32[]{:S(2)}, u32[]{:S(2)}) async-start(f32[16,32,256]{2,1,0:T(8,128)} %stack.30), calls=%async_computation.3 | async-start | bytes 1048576 | tf_op jit(solution)/shard_map/all_to_all | solution.py:19
  162.4 76.1 %collective-permute-start.7 = (bf16[512,3072]{1,0:T(8,128)(2,1)}, bf16[512,3072]{1,0:T(8,128)(2,1)}, u32[]{:S(2)}, u32[]{:S(2)}) collective-permute-start(bf16[512,3072]{1,0:T(8,128)(2,1)} %pad_maximum_fusion.1), channel_id=1, source_target_pairs={{0,64},{16,80},{32,96},{48,112},{64,0},{80,16},{96,32},{112,48},{1... | collective-permute-start | bytes 9437192 | tf_op jit(solution)/shard_map/ppermute | solution.py:41
  224.9 13.6 %collective-permute-start.6 = (bf16[256,512]{1,0:T(8,128)(2,1)S(1)}, bf16[256,512]{1,0:T(8,128)(2,1)S(1)}, u32[]{:S(2)}, u32[]{:S(2)}) collective-permute-start(bf16[256,512]{1,0:T(8,128)(2,1)S(1)} %fusion.21), channel_id=1, source_target_pairs={{0,64},{16,80},{32,96},{48,112},{64,0},{80,16},{96,32},{112,48},{1... | collective-permute-start | bytes 786440 | tf_op jit(solution)/shard_map/ppermute | solution.py:41
  228.7 14.6 %copy-start.1 = (bf16[256,3072]{1,0:T(8,128)(2,1)}, bf16[256,3072]{1,0:T(8,128)(2,1)S(1)}, u32[]{:S(2)}) copy-start(bf16[256,3072]{1,0:T(8,128)(2,1)S(1)} %convolution_convert_fusion.3) | copy-start | bytes 4718596
  262.7 20.2 %all-to-all-start.5 = ((f32[16,32,256]{2,1,0:T(8,128)}), f32[16,32,256]{2,1,0:T(8,128)S(1)}, u32[]{:S(2)}, u32[]{:S(2)}) async-start(f32[16,32,256]{2,1,0:T(8,128)} %stack.31), calls=%async_computation.5 | async-start | bytes 1048576 | tf_op jit(solution)/shard_map/all_to_all | solution.py:19
  269.4 77.4 %collective-permute-start.9 = (bf16[512,3072]{1,0:T(8,128)(2,1)}, bf16[512,3072]{1,0:T(8,128)(2,1)}, u32[]{:S(2)}, u32[]{:S(2)}) collective-permute-start(bf16[512,3072]{1,0:T(8,128)(2,1)} %pad_maximum_fusion.2), channel_id=1, source_target_pairs={{0,128},{16,144},{32,160},{48,176},{64,192},{80,208},{96,224},{112... | collective-permute-start | bytes 9437192 | tf_op jit(solution)/shard_map/ppermute | solution.py:41
  332.1 14.7 %collective-permute-start.8 = (bf16[256,512]{1,0:T(8,128)(2,1)S(1)}, bf16[256,512]{1,0:T(8,128)(2,1)S(1)}, u32[]{:S(2)}, u32[]{:S(2)}) collective-permute-start(bf16[256,512]{1,0:T(8,128)(2,1)S(1)} %fusion.22), channel_id=1, source_target_pairs={{0,128},{16,144},{32,160},{48,176},{64,192},{80,208},{96,224},{112... | collective-permute-start | bytes 786440 | tf_op jit(solution)/shard_map/ppermute | solution.py:41
  337.6 14.0 %copy-start.4 = (bf16[256,3072]{1,0:T(8,128)(2,1)}, bf16[256,3072]{1,0:T(8,128)(2,1)S(1)}, u32[]{:S(2)}) copy-start(bf16[256,3072]{1,0:T(8,128)(2,1)S(1)} %convolution_convert_fusion.1) | copy-start | bytes 4718596
  371.0 20.2 %all-to-all-start.7 = ((f32[16,32,256]{2,1,0:T(8,128)}), f32[16,32,256]{2,1,0:T(8,128)S(1)}, u32[]{:S(2)}, u32[]{:S(2)}) async-start(f32[16,32,256]{2,1,0:T(8,128)} %stack.32), calls=%async_computation.7 | async-start | bytes 1048576 | tf_op jit(solution)/shard_map/all_to_all | solution.py:19
